TPU v7x, 32 devices: a whole 2x2x4 slice. The times are simulated.
32 devices in a mesh: dp: 4 (over z), vocab: 8 (over y, x, core).
Axes of the slice: x: 2, y: 2, z: 4, core: 2. Of those that a mesh axis runs over, the one named last changes fastest.
Arguments:
- hidden: bfloat16 [512, 8192], P('dp', 'vocab'), may hold values from -8 to 8
- out_weight: bfloat16 [19456, 8192], P('vocab', 'dp'), may hold values from -0.397747564 to 0.397747564
- token_blocks: int32 [8, 4, 16], P('vocab'), may hold values from 0 to 18, as said below
- counts: int32 [8, 4], P('vocab'), may hold values from 4 to 16, as said below
Outputs:
- allowed_logprob: float32 [8, 4, 16, 128, 128], P('vocab', 'dp')
- expected: float32 [512, 8192], P('vocab', 'dp')
Inputs may be any that keep to these rules, and one draw needn't show every extreme that they name: token_blocks[j, b, s] names one of the 19 token blocks of shard j; the entries of one list are distinct; slots at or past counts[j, b] carry no meaning. `counts`: for every beam block, some shard allows exactly 16 slots.
All inputs are finite; a program needn't handle non-finite values.
Results may differ from a plain program's by a relative error of at most 0.0021.
Values may be sent and summed in bfloat16 or wider, within the bound.
No kernel may reach another device: no remote copies, remote signals or barrier semaphores. Data moves between devices by JAX's collectives and lax.ppermute only.
A program may use at most 128 MiB of HBM per device.

v0:
```python
import jax
import jax.numpy as jnp
from jax import lax
from jax.sharding import PartitionSpec as P

D = 8192
TB = 128
BB = 128
MOST = 16


def per_device(hidden, out_weight, token_blocks, counts):
    beams_here = hidden.shape[0]
    vocab_here, columns_here = out_weight.shape
    own_blocks = beams_here // BB
    block_lists = token_blocks[0]
    block_counts = counts[0]
    weight_blocks = out_weight.reshape(vocab_here // TB, TB, columns_here)
    first_block = lax.axis_index("dp") * own_blocks
    own_counts = lax.dynamic_slice_in_dim(block_counts, first_block, own_blocks, 0)
    beam_rows = lax.all_gather(hidden, "vocab", axis=1, tiled=True)
    beam_columns = lax.all_to_all(beam_rows, "dp", split_axis=1, concat_axis=0, tiled=True)
    column_blocks = beam_columns.reshape(-1, BB, columns_here)
    pick_part = block_lists

    def partial_one_block(pair_in):
        return jnp.einsum(
            "rd,std->srt", pair_in[0], weight_blocks[pair_in[1]], preferred_element_type=jnp.float32
        )

    logits = lax.psum_scatter(
        lax.map(partial_one_block, (column_blocks, pick_part)),
        "dp",
        scatter_dimension=0,
        tiled=True,
    )
    live = jnp.arange(MOST, dtype=jnp.int32)[None, :] < own_counts[:, None]
    live_mask = live[:, :, None, None]
    masked = jnp.where(live_mask, logits, -jnp.inf)
    local_max = jnp.max(masked, axis=(1, 3))
    beam_max = lax.pmax(local_max, "vocab")
    local_total = jnp.sum(jnp.exp(masked - beam_max[:, None, :, None]), axis=(1, 3))
    beam_total = lax.psum(local_total, "vocab")
    shifted = logits - beam_max[:, None, :, None] - jnp.log(beam_total)[:, None, :, None]
    allowed_logprob = jnp.where(live_mask, shifted, 0.0)
    probabilities = jnp.where(live_mask, jnp.exp(shifted), 0.0).astype(jnp.bfloat16)
    prob_part = lax.all_gather(probabilities, "dp", axis=0, tiled=True)
    block_count = prob_part.shape[0]
    pick_part = block_lists

    def expected_one_block(pair_in):
        return jnp.einsum(
            "srt,std->rd", pair_in[0], weight_blocks[pair_in[1]], preferred_element_type=jnp.float32
        )

    embedding_part = lax.map(expected_one_block, (prob_part, pick_part)).reshape(
        block_count * BB, columns_here
    )
    summed = lax.psum_scatter(embedding_part, "vocab", scatter_dimension=0, tiled=True)
    squares = lax.psum(jnp.sum(summed * summed, axis=1), "dp")
    expected = summed * lax.rsqrt(squares / D + 1e-06)[:, None]
    return (allowed_logprob[None], expected)


def solution(mesh):
    in_specs = (P("dp", "vocab"), P("vocab", "dp"), P("vocab", None, None), P("vocab", None))
    out_specs = (P("vocab", "dp", None, None, None), P("vocab", "dp"))
    return jax.shard_map(
        per_device, mesh=mesh, in_specs=in_specs, out_specs=out_specs, check_vma=False
    )
```

profile of v0, /device:TPU:0, one launch (start us, length us, event | category | flops | bytes accessed | tf_op | source)
XLA Modules:
  0.0 437.9 jit_solution(15092039008348145845)
XLA Ops:
  9.1 31.9 %all-gather.3.cloned.1.call-done = bf16[128,8192]{0,1:T(8,128)(2,1)} async-done(((bf16[128,1024]{0,1:T(8,128)(2,1)}), bf16[128,8192]{0,1:T(8,128)(2,1)}) %all-gather.3.cloned.1.call-update) | async-done | bytes 2097168 | tf_op jit(solution)/shard_map/all_gather | solution.py:21
  45.6 48.8 %all-to-all-done = bf16[128,4,2048]{0,2,1:T(8,128)(2,1)} async-done(((bf16[128,4,2048]{0,2,1:T(8,128)(2,1)}), bf16[128,4,2048]{0,2,1:T(8,128)(2,1)}, u32[]{:S(2)}, u32[]{:S(2)}) %all-to-all-start) | async-done | bytes 2097184 | tf_op jit(solution)/shard_map/all_to_all | solution.py:22
  94.4 63.4 %while.20 = (s32[]{:T(128)}, f32[4,16,128,128]{3,2,1,0:T(8,128)}, s32[4,16]{1,0:T(4,128)S(1)}, bf16[19,128,2048]{2,1,0:T(8,128)(2,1)}, bf16[4,128,2048]{1,2,0:T(8,128)(2,1)}, /*index=5*/s32[]{:T(128)}) while((s32[]{:T(128)}, f32[4,16,128,128]{3,2,1,0:T(8,128)}, s32[4,16]{1,0:T(4,128)S(1)}, bf16[19,128,2048]{2,1,0:T(8,128)(2,1)}, ...), condition=%wide.region_1.2_spmd, body=%wide.region_0.1_spmd.sunk | while | flops 1073742848 | bytes 30938440 | solution.py:32
  94.4 8.6 %gather_fusion = bf16[16,128,2048]{2,1,0:T(8,128)(2,1)} fusion(bf16[19,128,2048]{2,1,0:T(8,128)(2,1)} %get-tuple-element.167, s32[1024]{0:T(1024)S(1)} %pad_clamp_fusion.4), kind=kCustom, calls=%fused_computation.clone.1 | custom fusion | bytes 16777280 | tf_op jit(solution)/shard_map/while/body/eval_jaxpr/gather | solution.py:28
  103.0 5.8 %convolution_bitcast_fusion.3 = f32[1,16,128,128]{2,3,1,0:T(8,128)S(1)} fusion(bf16[16,128,2048]{2,1,0:T(8,128)(2,1)} %gather_fusion, bf16[4,128,2048]{1,2,0:T(8,128)(2,1)} %get-tuple-element.168, s32[]{:T(128)} %get-tuple-element.158), kind=kOutput, calls=%fused_computation.2.clone.1 | convolution fusion | flops 1073741824 | bytes 9961984 | tf_op jit(solution)/shard_map/while/body/eval_jaxpr/rd,std->srt/dot_general | solution.py:27
  110.4 8.6 %gather_fusion = bf16[16,128,2048]{2,1,0:T(8,128)(2,1)} fusion(bf16[19,128,2048]{2,1,0:T(8,128)(2,1)} %get-tuple-element.167, s32[1024]{0:T(1024)S(1)} %pad_clamp_fusion.4), kind=kCustom, calls=%fused_computation.clone.1 | custom fusion | bytes 16777280 | tf_op jit(solution)/shard_map/while/body/eval_jaxpr/gather | solution.py:28
  119.0 5.8 %convolution_bitcast_fusion.3 = f32[1,16,128,128]{2,3,1,0:T(8,128)S(1)} fusion(bf16[16,128,2048]{2,1,0:T(8,128)(2,1)} %gather_fusion, bf16[4,128,2048]{1,2,0:T(8,128)(2,1)} %get-tuple-element.168, s32[]{:T(128)} %get-tuple-element.158), kind=kOutput, calls=%fused_computation.2.clone.1 | convolution fusion | flops 1073741824 | bytes 9961984 | tf_op jit(solution)/shard_map/while/body/eval_jaxpr/rd,std->srt/dot_general | solution.py:27
  126.2 8.6 %gather_fusion = bf16[16,128,2048]{2,1,0:T(8,128)(2,1)} fusion(bf16[19,128,2048]{2,1,0:T(8,128)(2,1)} %get-tuple-element.167, s32[1024]{0:T(1024)S(1)} %pad_clamp_fusion.4), kind=kCustom, calls=%fused_computation.clone.1 | custom fusion | bytes 16777280 | tf_op jit(solution)/shard_map/while/body/eval_jaxpr/gather | solution.py:28
  134.8 5.8 %convolution_bitcast_fusion.3 = f32[1,16,128,128]{2,3,1,0:T(8,128)S(1)} fusion(bf16[16,128,2048]{2,1,0:T(8,128)(2,1)} %gather_fusion, bf16[4,128,2048]{1,2,0:T(8,128)(2,1)} %get-tuple-element.168, s32[]{:T(128)} %get-tuple-element.158), kind=kOutput, calls=%fused_computation.2.clone.1 | convolution fusion | flops 1073741824 | bytes 9961984 | tf_op jit(solution)/shard_map/while/body/eval_jaxpr/rd,std->srt/dot_general | solution.py:27
  142.0 8.6 %gather_fusion = bf16[16,128,2048]{2,1,0:T(8,128)(2,1)} fusion(bf16[19,128,2048]{2,1,0:T(8,128)(2,1)} %get-tuple-element.167, s32[1024]{0:T(1024)S(1)} %pad_clamp_fusion.4), kind=kCustom, calls=%fused_computation.clone.1 | custom fusion | bytes 16777280 | tf_op jit(solution)/shard_map/while/body/eval_jaxpr/gather | solution.py:28
  150.6 5.8 %convolution_bitcast_fusion.3 = f32[1,16,128,128]{2,3,1,0:T(8,128)S(1)} fusion(bf16[16,128,2048]{2,1,0:T(8,128)(2,1)} %gather_fusion, bf16[4,128,2048]{1,2,0:T(8,128)(2,1)} %get-tuple-element.168, s32[]{:T(128)} %get-tuple-element.158), kind=kOutput, calls=%fused_computation.2.clone.1 | convolution fusion | flops 1073741824 | bytes 9961984 | tf_op jit(solution)/shard_map/while/body/eval_jaxpr/rd,std->srt/dot_general | solution.py:27
  159.2 73.7 %reduce-scatter.3.cloned.1.call-done = f32[1,16,128,128]{3,2,1,0:T(8,128)} async-done(((f32[4,16,128,128]{3,2,1,0:T(8,128)}), f32[1,16,128,128]{3,2,1,0:T(8,128)}) %reduce-scatter.3.cloned.1.call-update) | async-done | bytes 1048592 | tf_op jit(solution)/shard_map/reduce_scatter | solution.py:31
  234.3 13.3 %pmax.7 = f32[128]{0:T(128)S(1)} all-reduce(f32[128]{0:T(128)S(1)} %select_reduce_fusion), channel_id=1, replica_groups=mesh['dp'=4,'vocab'=8] {'vocab'}, use_global_device_ids=true, to_apply=%region_4.5 | all-reduce | flops 128 | bytes 1024 | tf_op jit(solution)/shard_map/pmax | solution.py:41
  249.2 11.8 %psum.14 = f32[1,128]{1,0:T(1,128)S(1)} all-reduce(f32[1,128]{1,0:T(1,128)S(1)} %bitcast.69), channel_id=1, replica_groups=mesh['dp'=4,'vocab'=8] {'vocab'}, use_global_device_ids=true, to_apply=%region_6.7 | all-reduce | flops 128 | bytes 1024 | tf_op jit(solution)/shard_map/psum | solution.py:43
  263.9 44.7 %all-gather.5.cloned.1.call-done = bf16[4,16,128,128]{3,2,1,0:T(8,128)(2,1)} async-done(((bf16[1,16,128,128]{3,2,1,0:T(8,128)(2,1)}), bf16[4,16,128,128]{3,2,1,0:T(8,128)(2,1)}) %all-gather.5.cloned.1.call-update) | async-done | bytes 2097168 | tf_op jit(solution)/shard_map/all_gather | solution.py:47
  308.6 57.7 %while.21 = (s32[]{:T(128)}, f32[4,128,2048]{2,1,0:T(8,128)}, bf16[4,16,128,128]{3,2,1,0:T(8,128)(2,1)}, s32[4,16]{1,0:T(4,128)S(1)}, bf16[19,128,2048]{2,1,0:T(8,128)(2,1)}, /*index=5*/s32[]{:T(128)}) while((s32[]{:T(128)}, f32[4,128,2048]{2,1,0:T(8,128)}, bf16[4,16,128,128]{3,2,1,0:T(8,128)(2,1)}, s32[4,16]{1,0:T(4,128)S(1)}, ...), condition=%wide.region_8.9_spmd, body=%wide.region_7.8_spmd.sunk | while | flops 1073742848 | bytes 26744136 | solution.py:56
  308.7 8.6 %gather_fusion.1 = bf16[16,128,2048]{2,1,0:T(8,128)(2,1)} fusion(bf16[19,128,2048]{2,1,0:T(8,128)(2,1)} %get-tuple-element.186, s32[1024]{0:T(1024)S(1)} %pad_clamp_fusion.5), kind=kCustom, calls=%fused_computation.1.clone.1 | custom fusion | bytes 16777280 | tf_op jit(solution)/shard_map/while/body/eval_jaxpr/gather | solution.py:53
  317.3 5.9 %fusion.26 = f32[4,128,2048]{2,1,0:T(8,128)} fusion(f32[4,128,2048]{2,1,0:T(8,128)} %get-tuple-element.177, s32[]{:T(128)} %get-tuple-element.176, bf16[16,128,2048]{2,1,0:T(8,128)(2,1)} %gather_fusion.1, bf16[4,16,128,128]{3,2,1,0:T(8,128)(2,1)} %get-tuple-element.184), kind=kOutput, calls=%fused_computation.13.clone.1 | convolution fusion | flops 1073741824 | bytes 9962496 | tf_op jit(solution)/shard_map/while/body/eval_jaxpr/srt,std->rd/dot_general | solution.py:52
  323.2 8.6 %gather_fusion.1 = bf16[16,128,2048]{2,1,0:T(8,128)(2,1)} fusion(bf16[19,128,2048]{2,1,0:T(8,128)(2,1)} %get-tuple-element.186, s32[1024]{0:T(1024)S(1)} %pad_clamp_fusion.5), kind=kCustom, calls=%fused_computation.1.clone.1 | custom fusion | bytes 16777280 | tf_op jit(solution)/shard_map/while/body/eval_jaxpr/gather | solution.py:53
  337.6 8.6 %gather_fusion.1 = bf16[16,128,2048]{2,1,0:T(8,128)(2,1)} fusion(bf16[19,128,2048]{2,1,0:T(8,128)(2,1)} %get-tuple-element.186, s32[1024]{0:T(1024)S(1)} %pad_clamp_fusion.5), kind=kCustom, calls=%fused_computation.1.clone.1 | custom fusion | bytes 16777280 | tf_op jit(solution)/shard_map/while/body/eval_jaxpr/gather | solution.py:53
  346.2 5.8 %fusion.26 = f32[4,128,2048]{2,1,0:T(8,128)} fusion(f32[4,128,2048]{2,1,0:T(8,128)} %get-tuple-element.177, s32[]{:T(128)} %get-tuple-element.176, bf16[16,128,2048]{2,1,0:T(8,128)(2,1)} %gather_fusion.1, bf16[4,16,128,128]{3,2,1,0:T(8,128)(2,1)} %get-tuple-element.184), kind=kOutput, calls=%fused_computation.13.clone.1 | convolution fusion | flops 1073741824 | bytes 9962496 | tf_op jit(solution)/shard_map/while/body/eval_jaxpr/srt,std->rd/dot_general | solution.py:52
  352.0 8.6 %gather_fusion.1 = bf16[16,128,2048]{2,1,0:T(8,128)(2,1)} fusion(bf16[19,128,2048]{2,1,0:T(8,128)(2,1)} %get-tuple-element.186, s32[1024]{0:T(1024)S(1)} %pad_clamp_fusion.5), kind=kCustom, calls=%fused_computation.1.clone.1 | custom fusion | bytes 16777280 | tf_op jit(solution)/shard_map/while/body/eval_jaxpr/gather | solution.py:53
  366.4 50.1 %reduce-scatter.5.cloned.1.call-done = f32[64,2048]{1,0:T(8,128)} async-done(((f32[512,2048]{1,0:T(8,128)}), f32[64,2048]{1,0:T(8,128)}) %reduce-scatter.5.cloned.1.call-update) | async-done | bytes 524304 | tf_op jit(solution)/shard_map/reduce_scatter | solution.py:59
  417.7 11.7 %psum.15 = f32[64]{0:T(128)S(1)} all-reduce(f32[64]{0:T(128)S(1)} %multiply_reduce_fusion), channel_id=1, replica_groups=mesh['dp'=4,'vocab'=8] {'dp'}, use_global_device_ids=true, to_apply=%region_11.12 | all-reduce | flops 64 | bytes 512 | tf_op jit(solution)/shard_map/psum | solution.py:60
  (51 shorter events, 34.1 us)
Async XLA Ops:
  7.2 150.7 %copy-start = (s32[1,4]{1,0:T(1,128)S(1)}, s32[1,4]{1,0:T(1,128)}, u32[]{:S(2)}) copy-start(s32[1,4]{1,0:T(1,128)} %param.11) | copy-start | bytes 52
  7.2 87.2 %copy-start.1 = (s32[1,4,16]{2,1,0:T(4,128)S(1)}, s32[1,4,16]{2,1,0:T(4,128)}, u32[]{:S(2)}) copy-start(s32[1,4,16]{2,1,0:T(4,128)} %param.10) | copy-start | bytes 772
  7.2 33.8 %all-gather.3.cloned.1.call-start = ((), (), s32[]{:S(2)}) async-start(), calls=%async_computation.3 | async-start | bytes 2359296 | tf_op jit(solution)/shard_map/all_gather | solution.py:21
  41.0 53.4 %all-to-all-start = ((bf16[128,4,2048]{0,2,1:T(8,128)(2,1)}), bf16[128,4,2048]{0,2,1:T(8,128)(2,1)}, u32[]{:S(2)}, u32[]{:S(2)}) async-start(bf16[128,4,2048]{0,2,1:T(8,128)(2,1)} %bitcast.68), calls=%async_computation | async-start | bytes 4194304 | tf_op jit(solution)/shard_map/all_to_all | solution.py:22
  45.6 187.3 %reduce-scatter.3.cloned.1.call-start = ((), (), s32[]{:S(2)}) async-start(), calls=%async_computation.4 | async-start | bytes 5242880 | tf_op jit(solution)/shard_map/reduce_scatter | solution.py:31
  157.8 150.8 %all-gather.5.cloned.1.call-start = ((), (), s32[]{:S(2)}) async-start(), calls=%async_computation.5 | async-start | bytes 2621440 | tf_op jit(solution)/shard_map/all_gather | solution.py:47
  263.8 152.7 %reduce-scatter.5.cloned.1.call-start = ((), (), s32[]{:S(2)}) async-start(), calls=%async_computation.6 | async-start | bytes 4718592 | tf_op jit(solution)/shard_map/reduce_scatter | solution.py:59
Sparse Core Ops, SparseCore 0:
  10.5 30.4 all-gather.2
  158.0 74.8 reduce-scatter.2
  264.0 44.6 all-gather.4
  366.5 49.9 reduce-scatter.4
where the time goes:
time: 439 us; the launch traced here: 438 us
  waiting for transfers between devices  249 us (57%)
  local copies, waits for them, and re-layouts  76.8 us (17%)
  matrix products  46.6 us (11%)
  blocking collectives  36.8 us (8%)
  between operations  13.8 us (3%)
  other arithmetic  9.7 us (2%)
  starting transfers between devices  4.72 us (1%)
    reduce_scatter x1, waiting for transfers between devices, per_device(): lax.psum_scatter(lax.map(partial_one_block, (column_blocks, pick_part)),...  73.7 us
    reduce_scatter x1, waiting for transfers between devices, per_device(): lax.psum_scatter(embedding_part, 'vocab', scatter_dimension=0, tiled=True)  50.1 us
    all_to_all x1, waiting for transfers between devices, per_device(): lax.all_to_all(beam_rows, 'dp', split_axis=1, concat_axis=0, tiled=True)  48.8 us
    all_gather x1, waiting for transfers between devices, per_device(): prob_part = lax.all_gather(probabilities, 'dp', axis=0, tiled=True)  44.7 us
    gather x4, local copies, waits for them, and re-layouts, partial_one_block(): weight_blocks[pair_in[1]]  34.4 us
    gather x4, local copies, waits for them, and re-layouts, expected_one_block(): weight_blocks[pair_in[1]]  34.4 us
    all_gather x1, waiting for transfers between devices, per_device(): beam_rows = lax.all_gather(hidden, 'vocab', axis=1, tiled=True)  31.9 us
    dot_general x4, matrix products, expected_one_block(): jnp.einsum('srt,std->rd', pair_in[0], weight_blocks[pair_in[1]], preferre...  23.3 us
  transfers between devices with their start and end apart: 5, of which 5 were waited for; matrix products, arithmetic and copies ran while one was open for 0% of the time, Pallas kernels for 0%

commit v1 on v0

--- a/solution.py
+++ b/solution.py
@@ -7,6 +7,18 @@
 TB = 128
 BB = 128
 MOST = 16
+
+
+def collect(value, axis, dim):
+    ways, here = (lax.axis_size(axis), lax.axis_index(axis))
+    grown, reach = (value, 1)
+    while reach < ways:
+        theirs = lax.ppermute(grown, axis, [(d, d ^ reach) for d in range(ways)])
+        mine_first = jnp.concatenate([grown, theirs], axis=dim)
+        theirs_first = jnp.concatenate([theirs, grown], axis=dim)
+        grown = jnp.where(here & reach == 0, mine_first, theirs_first)
+        reach = 2 * reach
+    return grown
 
 
 def per_device(hidden, out_weight, token_blocks, counts):
@@ -44,7 +56,7 @@
     shifted = logits - beam_max[:, None, :, None] - jnp.log(beam_total)[:, None, :, None]
     allowed_logprob = jnp.where(live_mask, shifted, 0.0)
     probabilities = jnp.where(live_mask, jnp.exp(shifted), 0.0).astype(jnp.bfloat16)
-    prob_part = lax.all_gather(probabilities, "dp", axis=0, tiled=True)
+    prob_part = collect(probabilities, "dp", 0)
     block_count = prob_part.shape[0]
     pick_part = block_lists
 

time: 439 us -> 457 us (1.041)
  waiting for transfers between devices: 249 us -> 261 us
  starting transfers between devices: 4.72 us -> 9.69 us
    ppermute x0 -> x2, waiting for transfers between devices: none -> 56.9 us  [collect(): theirs = lax.ppermute(grown, axis, [(d, d ^ reach) for d in range(ways)])]
    all_gather x1 -> x0, waiting for transfers between devices: 44.7 us -> none  [per_device(): prob_part = lax.all_gather(probabilities, 'dp', axis=0, tiled=True)]
    ppermute x0 -> x2, starting transfers between devices: none -> 5.01 us  [collect(): theirs = lax.ppermute(grown, axis, [(d, d ^ reach) for d in range(ways)])]
  transfers between devices with their start and end apart: 5 -> 6, of which waited for: 5 -> 6; matrix products, arithmetic and copies ran while one was open for 0% -> 0% of each run, Pallas kernels for 0% -> 0%
where the time goes in v1:
time: 457 us; the launch traced here: 456 us
  waiting for transfers between devices  261 us (57%)
  local copies, waits for them, and re-layouts  76.8 us (17%)
  matrix products  46.2 us (10%)
  blocking collectives  36.8 us (8%)
  between operations  13.8 us (3%)
  other arithmetic  11.7 us (3%)
  starting transfers between devices  9.69 us (2%)
    reduce_scatter x1, waiting for transfers between devices, per_device(): lax.psum_scatter(lax.map(partial_one_block, (column_blocks, pick_part)),...  73.7 us
    ppermute x2, waiting for transfers between devices, collect(): theirs = lax.ppermute(grown, axis, [(d, d ^ reach) for d in range(ways)])  56.9 us
    reduce_scatter x1, waiting for transfers between devices, per_device(): lax.psum_scatter(embedding_part, 'vocab', scatter_dimension=0, tiled=True)  49.8 us
    all_to_all x1, waiting for transfers between devices, per_device(): lax.all_to_all(beam_rows, 'dp', split_axis=1, concat_axis=0, tiled=True)  48.8 us
    gather x4, local copies, waits for them, and re-layouts, expected_one_block(): weight_blocks[pair_in[1]]  34.4 us
    gather x4, local copies, waits for them, and re-layouts, partial_one_block(): weight_blocks[pair_in[1]]  34.4 us
    all_gather x1, waiting for transfers between devices, per_device(): beam_rows = lax.all_gather(hidden, 'vocab', axis=1, tiled=True)  31.9 us
    dot_general x4, matrix products, partial_one_block(): jnp.einsum('rd,std->srt', pair_in[0], weight_blocks[pair_in[1]], preferre...  23.3 us
  transfers between devices with their start and end apart: 6, of which 6 were waited for; matrix products, arithmetic and copies ran while one was open for 0% of the time, Pallas kernels for 0%

profile of v1, /device:TPU:0, one launch (start us, length us, event | category | flops | bytes accessed | tf_op | source)
XLA Modules:
  0.0 456.2 jit_solution(7752096361148741956)
XLA Ops:
  9.1 31.9 %all-gather.2.cloned.1.call-done = bf16[128,8192]{0,1:T(8,128)(2,1)} async-done(((bf16[128,1024]{0,1:T(8,128)(2,1)}), bf16[128,8192]{0,1:T(8,128)(2,1)}) %all-gather.2.cloned.1.call-update) | async-done | bytes 2097168 | tf_op jit(solution)/shard_map/all_gather | solution.py:33
  45.6 48.8 %all-to-all-done = bf16[128,4,2048]{0,2,1:T(8,128)(2,1)} async-done(((bf16[128,4,2048]{0,2,1:T(8,128)(2,1)}), bf16[128,4,2048]{0,2,1:T(8,128)(2,1)}, u32[]{:S(2)}, u32[]{:S(2)}) %all-to-all-start) | async-done | bytes 2097184 | tf_op jit(solution)/shard_map/all_to_all | solution.py:34
  94.4 63.4 %while.20 = (s32[]{:T(128)}, f32[4,16,128,128]{3,2,1,0:T(8,128)}, s32[4,16]{1,0:T(4,128)S(1)}, bf16[19,128,2048]{2,1,0:T(8,128)(2,1)}, bf16[4,128,2048]{1,2,0:T(8,128)(2,1)}, /*index=5*/s32[]{:T(128)}) while((s32[]{:T(128)}, f32[4,16,128,128]{3,2,1,0:T(8,128)}, s32[4,16]{1,0:T(4,128)S(1)}, bf16[19,128,2048]{2,1,0:T(8,128)(2,1)}, ...), condition=%wide.region_1.2_spmd, body=%wide.region_0.1_spmd.sunk | while | flops 1073742848 | bytes 30938440 | solution.py:44
  94.4 8.6 %gather_fusion = bf16[16,128,2048]{2,1,0:T(8,128)(2,1)} fusion(bf16[19,128,2048]{2,1,0:T(8,128)(2,1)} %get-tuple-element.162, s32[1024]{0:T(1024)S(1)} %pad_clamp_fusion.4), kind=kCustom, calls=%fused_computation.clone.1 | custom fusion | bytes 16777280 | tf_op jit(solution)/shard_map/while/body/eval_jaxpr/gather | solution.py:40
  103.0 5.8 %convolution_bitcast_fusion.3 = f32[1,16,128,128]{2,3,1,0:T(8,128)S(1)} fusion(bf16[16,128,2048]{2,1,0:T(8,128)(2,1)} %gather_fusion, bf16[4,128,2048]{1,2,0:T(8,128)(2,1)} %get-tuple-element.163, s32[]{:T(128)} %get-tuple-element.153), kind=kOutput, calls=%fused_computation.2.clone.1 | convolution fusion | flops 1073741824 | bytes 9961984 | tf_op jit(solution)/shard_map/while/body/eval_jaxpr/rd,std->srt/dot_general | solution.py:39
  110.4 8.6 %gather_fusion = bf16[16,128,2048]{2,1,0:T(8,128)(2,1)} fusion(bf16[19,128,2048]{2,1,0:T(8,128)(2,1)} %get-tuple-element.162, s32[1024]{0:T(1024)S(1)} %pad_clamp_fusion.4), kind=kCustom, calls=%fused_computation.clone.1 | custom fusion | bytes 16777280 | tf_op jit(solution)/shard_map/while/body/eval_jaxpr/gather | solution.py:40
  119.0 5.8 %convolution_bitcast_fusion.3 = f32[1,16,128,128]{2,3,1,0:T(8,128)S(1)} fusion(bf16[16,128,2048]{2,1,0:T(8,128)(2,1)} %gather_fusion, bf16[4,128,2048]{1,2,0:T(8,128)(2,1)} %get-tuple-element.163, s32[]{:T(128)} %get-tuple-element.153), kind=kOutput, calls=%fused_computation.2.clone.1 | convolution fusion | flops 1073741824 | bytes 9961984 | tf_op jit(solution)/shard_map/while/body/eval_jaxpr/rd,std->srt/dot_general | solution.py:39
  126.2 8.6 %gather_fusion = bf16[16,128,2048]{2,1,0:T(8,128)(2,1)} fusion(bf16[19,128,2048]{2,1,0:T(8,128)(2,1)} %get-tuple-element.162, s32[1024]{0:T(1024)S(1)} %pad_clamp_fusion.4), kind=kCustom, calls=%fused_computation.clone.1 | custom fusion | bytes 16777280 | tf_op jit(solution)/shard_map/while/body/eval_jaxpr/gather | solution.py:40
  134.8 5.8 %convolution_bitcast_fusion.3 = f32[1,16,128,128]{2,3,1,0:T(8,128)S(1)} fusion(bf16[16,128,2048]{2,1,0:T(8,128)(2,1)} %gather_fusion, bf16[4,128,2048]{1,2,0:T(8,128)(2,1)} %get-tuple-element.163, s32[]{:T(128)} %get-tuple-element.153), kind=kOutput, calls=%fused_computation.2.clone.1 | convolution fusion | flops 1073741824 | bytes 9961984 | tf_op jit(solution)/shard_map/while/body/eval_jaxpr/rd,std->srt/dot_general | solution.py:39
  142.0 8.6 %gather_fusion = bf16[16,128,2048]{2,1,0:T(8,128)(2,1)} fusion(bf16[19,128,2048]{2,1,0:T(8,128)(2,1)} %get-tuple-element.162, s32[1024]{0:T(1024)S(1)} %pad_clamp_fusion.4), kind=kCustom, calls=%fused_computation.clone.1 | custom fusion | bytes 16777280 | tf_op jit(solution)/shard_map/while/body/eval_jaxpr/gather | solution.py:40
  150.6 5.8 %convolution_bitcast_fusion.3 = f32[1,16,128,128]{2,3,1,0:T(8,128)S(1)} fusion(bf16[16,128,2048]{2,1,0:T(8,128)(2,1)} %gather_fusion, bf16[4,128,2048]{1,2,0:T(8,128)(2,1)} %get-tuple-element.163, s32[]{:T(128)} %get-tuple-element.153), kind=kOutput, calls=%fused_computation.2.clone.1 | convolution fusion | flops 1073741824 | bytes 9961984 | tf_op jit(solution)/shard_map/while/body/eval_jaxpr/rd,std->srt/dot_general | solution.py:39
  159.2 73.7 %reduce-scatter.3.cloned.1.call-done = f32[1,16,128,128]{3,2,1,0:T(8,128)} async-done(((f32[4,16,128,128]{3,2,1,0:T(8,128)}), f32[1,16,128,128]{3,2,1,0:T(8,128)}) %reduce-scatter.3.cloned.1.call-update) | async-done | bytes 1048592 | tf_op jit(solution)/shard_map/reduce_scatter | solution.py:43
  234.3 13.3 %pmax.7 = f32[128]{0:T(128)S(1)} all-reduce(f32[128]{0:T(128)S(1)} %select_reduce_fusion), channel_id=1, replica_groups=mesh['dp'=4,'vocab'=8] {'vocab'}, use_global_device_ids=true, to_apply=%region_4.5 | all-reduce | flops 128 | bytes 1024 | tf_op jit(solution)/shard_map/pmax | solution.py:53
  249.2 11.8 %psum.14 = f32[1,128]{1,0:T(1,128)S(1)} all-reduce(f32[1,128]{1,0:T(1,128)S(1)} %bitcast.69), channel_id=1, replica_groups=mesh['dp'=4,'vocab'=8] {'vocab'}, use_global_device_ids=true, to_apply=%region_6.7 | all-reduce | flops 128 | bytes 1024 | tf_op jit(solution)/shard_map/psum | solution.py:55
  265.4 12.0 %collective-permute-done = bf16[1,16,128,128]{3,2,1,0:T(8,128)(2,1)S(1)} collective-permute-done((bf16[1,16,128,128]{3,2,1,0:T(8,128)(2,1)S(1)}, bf16[1,16,128,128]{3,2,1,0:T(8,128)(2,1)S(1)}, u32[]{:S(2)}, u32[]{:S(2)}) %collective-permute-start) | collective-permute-done | bytes 524320 | tf_op jit(solution)/shard_map/ppermute | solution.py:16
  280.8 44.9 %collective-permute-done.1 = bf16[2,16,128,128]{3,2,1,0:T(8,128)(2,1)} collective-permute-done((bf16[2,16,128,128]{3,2,1,0:T(8,128)(2,1)S(1)}, bf16[2,16,128,128]{3,2,1,0:T(8,128)(2,1)}, u32[]{:S(2)}, u32[]{:S(2)}) %collective-permute-start.1) | collective-permute-done | bytes 1048608 | tf_op jit(solution)/shard_map/ppermute | solution.py:16
  327.7 57.4 %while.21 = (s32[]{:T(128)}, f32[4,128,2048]{2,1,0:T(8,128)}, bf16[4,16,128,128]{3,2,1,0:T(8,128)(2,1)S(1)}, s32[4,16]{1,0:T(4,128)S(1)}, bf16[19,128,2048]{2,1,0:T(8,128)(2,1)}, /*index=5*/s32[]{:T(128)}) while((s32[]{:T(128)}, f32[4,128,2048]{2,1,0:T(8,128)}, bf16[4,16,128,128]{3,2,1,0:T(8,128)(2,1)S(1)}, s32[4,16]{1,0:T(4,128)S(1)}, ...), condition=%wide.region_8.9_spmd, body=%wide.region_7.8_spmd.sunk | while | flops 1073742848 | bytes 26744136 | solution.py:68
  327.7 8.6 %gather_fusion.1 = bf16[16,128,2048]{2,1,0:T(8,128)(2,1)} fusion(bf16[19,128,2048]{2,1,0:T(8,128)(2,1)} %get-tuple-element.181, s32[1024]{0:T(1024)S(1)} %pad_clamp_fusion.5), kind=kCustom, calls=%fused_computation.1.clone.1 | custom fusion | bytes 16777280 | tf_op jit(solution)/shard_map/while/body/eval_jaxpr/gather | solution.py:65
  336.3 5.8 %fusion.26 = f32[4,128,2048]{2,1,0:T(8,128)} fusion(f32[4,128,2048]{2,1,0:T(8,128)} %get-tuple-element.172, s32[]{:T(128)} %get-tuple-element.171, bf16[16,128,2048]{2,1,0:T(8,128)(2,1)} %gather_fusion.1, bf16[4,16,128,128]{3,2,1,0:T(8,128)(2,1)S(1)} %get-tuple-element.179), kind=kOutput, calls=%fused_computation.13.clone.1 | convolution fusion | flops 1073741824 | bytes 9962496 | tf_op jit(solution)/shard_map/while/body/eval_jaxpr/srt,std->rd/dot_general | solution.py:64
  342.1 8.6 %gather_fusion.1 = bf16[16,128,2048]{2,1,0:T(8,128)(2,1)} fusion(bf16[19,128,2048]{2,1,0:T(8,128)(2,1)} %get-tuple-element.181, s32[1024]{0:T(1024)S(1)} %pad_clamp_fusion.5), kind=kCustom, calls=%fused_computation.1.clone.1 | custom fusion | bytes 16777280 | tf_op jit(solution)/shard_map/while/body/eval_jaxpr/gather | solution.py:65
  356.4 8.6 %gather_fusion.1 = bf16[16,128,2048]{2,1,0:T(8,128)(2,1)} fusion(bf16[19,128,2048]{2,1,0:T(8,128)(2,1)} %get-tuple-element.181, s32[1024]{0:T(1024)S(1)} %pad_clamp_fusion.5), kind=kCustom, calls=%fused_computation.1.clone.1 | custom fusion | bytes 16777280 | tf_op jit(solution)/shard_map/while/body/eval_jaxpr/gather | solution.py:65
  370.8 8.6 %gather_fusion.1 = bf16[16,128,2048]{2,1,0:T(8,128)(2,1)} fusion(bf16[19,128,2048]{2,1,0:T(8,128)(2,1)} %get-tuple-element.181, s32[1024]{0:T(1024)S(1)} %pad_clamp_fusion.5), kind=kCustom, calls=%fused_computation.1.clone.1 | custom fusion | bytes 16777280 | tf_op jit(solution)/shard_map/while/body/eval_jaxpr/gather | solution.py:65
  385.1 49.8 %reduce-scatter.5.cloned.1.call-done = f32[64,2048]{1,0:T(8,128)} async-done(((f32[512,2048]{1,0:T(8,128)}), f32[64,2048]{1,0:T(8,128)}) %reduce-scatter.5.cloned.1.call-update) | async-done | bytes 524304 | tf_op jit(solution)/shard_map/reduce_scatter | solution.py:71
  436.0 11.7 %psum.15 = f32[64]{0:T(128)S(1)} all-reduce(f32[64]{0:T(128)S(1)} %multiply_reduce_fusion), channel_id=1, replica_groups=mesh['dp'=4,'vocab'=8] {'dp'}, use_global_device_ids=true, to_apply=%region_11.12 | all-reduce | flops 64 | bytes 512 | tf_op jit(solution)/shard_map/psum | solution.py:72
  (54 shorter events, 46.6 us)
Async XLA Ops:
  7.2 150.7 %copy-start = (s32[1,4]{1,0:T(1,128)S(1)}, s32[1,4]{1,0:T(1,128)}, u32[]{:S(2)}) copy-start(s32[1,4]{1,0:T(1,128)} %param.11) | copy-start | bytes 52
  7.2 87.2 %copy-start.1 = (s32[1,4,16]{2,1,0:T(4,128)S(1)}, s32[1,4,16]{2,1,0:T(4,128)}, u32[]{:S(2)}) copy-start(s32[1,4,16]{2,1,0:T(4,128)} %param.10) | copy-start | bytes 772
  7.2 33.8 %all-gather.2.cloned.1.call-start = ((), (), s32[]{:S(2)}) async-start(), calls=%async_computation.3 | async-start | bytes 2359296 | tf_op jit(solution)/shard_map/all_gather | solution.py:33
  41.0 53.4 %all-to-all-start = ((bf16[128,4,2048]{0,2,1:T(8,128)(2,1)}), bf16[128,4,2048]{0,2,1:T(8,128)(2,1)}, u32[]{:S(2)}, u32[]{:S(2)}) async-start(bf16[128,4,2048]{0,2,1:T(8,128)(2,1)} %bitcast.68), calls=%async_computation | async-start | bytes 4194304 | tf_op jit(solution)/shard_map/all_to_all | solution.py:34
  45.6 187.3 %reduce-scatter.3.cloned.1.call-start = ((), (), s32[]{:S(2)}) async-start(), calls=%async_computation.4 | async-start | bytes 5242880 | tf_op jit(solution)/shard_map/reduce_scatter | solution.py:43
  157.8 277.0 %reduce-scatter.5.cloned.1.call-start = ((), (), s32[]{:S(2)}) async-start(), calls=%async_computation.5 | async-start | bytes 4718592 | tf_op jit(solution)/shard_map/reduce_scatter | solution.py:71
  263.7 13.7 %collective-permute-start = (bf16[1,16,128,128]{3,2,1,0:T(8,128)(2,1)S(1)}, bf16[1,16,128,128]{3,2,1,0:T(8,128)(2,1)S(1)}, u32[]{:S(2)}, u32[]{:S(2)}) collective-permute-start(bf16[1,16,128,128]{3,2,1,0:T(8,128)(2,1)S(1)} %get-tuple-element.83), channel_id=1, source_target_pairs={{0,8},{8,0},{16,24},{24,16},{1,9},{9,1},{17,25},{25,17},{2,10},{10... | collective-permute-start | bytes 1572872 | tf_op jit(solution)/shard_map/ppermute | solution.py:16
  277.5 48.2 %collective-permute-start.1 = (bf16[2,16,128,128]{3,2,1,0:T(8,128)(2,1)S(1)}, bf16[2,16,128,128]{3,2,1,0:T(8,128)(2,1)}, u32[]{:S(2)}, u32[]{:S(2)}) collective-permute-start(bf16[2,16,128,128]{3,2,1,0:T(8,128)(2,1)S(1)} %maximum_select_fusion.1), channel_id=1, source_target_pairs={{0,16},{8,24},{16,0},{24,8},{1,17},{9,25},{17,1},{25,9},{2,18},{10... | collective-permute-start | bytes 3145736 | tf_op jit(solution)/shard_map/ppermute | solution.py:16
Sparse Core Ops, SparseCore 0:
  10.5 30.4 all-gather.1
  158.0 74.8 reduce-scatter.2
  385.2 49.5 reduce-scatter.4
